TPU v7x, 32 devices: a whole 2x2x4 slice. The times are simulated.
32 devices in a mesh: wide: 16 (over z, y, x), narrow: 2 (over core).
Axes of the slice: x: 2, y: 2, z: 4, core: 2. Of those that a mesh axis runs over, the one named last changes fastest.
Arguments:
- sample_t: float32 [512, 65536], P(('wide', 'narrow')), may hold values from -300 to 300
Outputs:
- basis: float32 [65536, 512], P(('wide', 'narrow'))
- factor_out: float32 [512, 512], replicated
All inputs are finite; a program needn't handle non-finite values.
Results may differ from a plain program's by a relative error of at most 0.000084.
Values sent between devices are 32-bit elements; how exact they have to be, the bound alone decides.
No kernel may reach another device: no remote copies, remote signals or barrier semaphores. Data moves between devices by JAX's collectives and lax.ppermute only.
A program may use at most 64 MiB of HBM per device.

v0:
```python
import math
import jax
import jax.numpy as jnp
from jax import lax
from jax.sharding import PartitionSpec as P

AXES = ("wide", "narrow")


def _mm(a, b):
    return jnp.dot(a, b, precision=lax.Precision.HIGHEST, preferred_element_type=jnp.float32)


def _diag_pair(block):
    lower = lax.linalg.cholesky(block)
    identity = jnp.eye(block.shape[0], dtype=block.dtype)
    solved = lax.linalg.triangular_solve(lower, identity, left_side=True, lower=True)
    return (lower, solved)


def factor_pair(matrix, b=128):
    n = matrix.shape[0]
    nb = n // b
    trail = matrix
    l_blk = {}
    d_inv = []
    for k in range(nb):
        l_kk, i_kk = _diag_pair(trail[:b, :b])
        d_inv.append(i_kk)
        l_blk[k, k] = l_kk
        if k < nb - 1:
            panel = _mm(trail[b:, :b], i_kk.T)
            for i in range(k + 1, nb):
                l_blk[i, k] = panel[(i - k - 1) * b : (i - k) * b]
            trail = trail[b:, b:] - _mm(panel, panel.T)
    inv = {}
    for j in range(nb):
        inv[j, j] = d_inv[j]
        for i in range(j + 1, nb):
            acc = _mm(l_blk[i, j], inv[j, j])
            for m in range(j + 1, i):
                acc = acc + _mm(l_blk[i, m], inv[m, j])
            inv[i, j] = -_mm(d_inv[i], acc)
    zero = jnp.zeros((b, b), matrix.dtype)
    lower = jnp.concatenate(
        [jnp.concatenate([l_blk.get((i, j), zero) for j in range(nb)], 1) for i in range(nb)], 0
    )
    lower_inv = jnp.concatenate(
        [jnp.concatenate([inv.get((i, j), zero) for j in range(nb)], 1) for i in range(nb)], 0
    )
    return (lower, lower_inv)


def _pair(count, bit):
    return [(i, i ^ bit) for i in range(count)]


def sum_by_halving(local, count):
    steps = count.bit_length() - 1
    assert 1 << steps == count and local.shape[0] % count == 0
    idx = lax.axis_index(AXES)
    buf = local
    for k in range(steps):
        half = buf.shape[0] // 2
        b = idx >> k & 1
        keep = lax.dynamic_slice_in_dim(buf, b * half, half, 0)
        send = lax.dynamic_slice_in_dim(buf, (1 - b) * half, half, 0)
        buf = keep + lax.ppermute(send, AXES, _pair(count, 1 << k))
    for k in reversed(range(steps)):
        b = idx >> k & 1
        recv = lax.ppermute(buf, AXES, _pair(count, 1 << k))
        lo = jnp.where(b == 0, buf, recv)
        hi = jnp.where(b == 0, recv, buf)
        buf = jnp.concatenate([lo, hi], 0)
    return buf


def per_device(sample_t):
    wide_count = lax.axis_size("wide")
    narrow_count = lax.axis_size("narrow")
    count = wide_count * narrow_count
    rows_t = lax.all_to_all(sample_t, AXES, split_axis=1, concat_axis=0, tiled=True)
    gram_local = jnp.dot(
        rows_t, rows_t.T, precision=lax.Precision.HIGHEST, preferred_element_type=jnp.float32
    )
    gram_total = sum_by_halving(gram_local, count)
    lower, lower_inv = factor_pair(gram_total)
    upper_factor = lower.T
    inverse = lower_inv.T
    total_rows = rows_t.shape[1] * count
    scale_root = math.sqrt(total_rows)
    product = lax.dot_general(
        rows_t,
        inverse,
        (((0,), (0,)), ((), ())),
        precision=lax.Precision.HIGHEST,
        preferred_element_type=jnp.float32,
    )
    return (product * scale_root, upper_factor / scale_root)


def solution(mesh):
    in_specs = (P(AXES, None),)
    out_specs = (P(AXES, None), P())
    return jax.shard_map(
        per_device, mesh=mesh, in_specs=in_specs, out_specs=out_specs, check_vma=False
    )
```

profile of v0, /device:TPU:0, one launch (start us, length us, event | category | flops | bytes accessed | tf_op | source)
XLA Modules:
  0.0 287.7 jit_solution(4122485212012799821)
XLA Ops:
  0.6 4.7 %copy.140 = f32[2,32,8,2048]{3,2,0,1:T(8,128)} copy(f32[2,32,8,2048]{3,2,1,0:T(8,128)} %bitcast.83) | data formatting | bytes 8388608 | tf_op jit(solution)/shard_map/all_to_all | solution.py:82
  5.3 7.4 %all-to-all-start = ((f32[16,32,2048]{2,0,1:T(8,128)}), f32[16,32,2048]{2,0,1:T(8,128)}, u32[]{:S(2)}, u32[]{:S(2)}) async-start(f32[16,32,2048]{2,0,1:T(8,128)} %bitcast.82), calls=%async_computation | async-start | bytes 8388608 | tf_op jit(solution)/shard_map/all_to_all | solution.py:82
  12.8 93.9 %all-to-all-done = f32[16,32,2048]{2,0,1:T(8,128)} async-done(((f32[16,32,2048]{2,0,1:T(8,128)}), f32[16,32,2048]{2,0,1:T(8,128)}, u32[]{:S(2)}, u32[]{:S(2)}) %all-to-all-start) | async-done | bytes 4194336 | tf_op jit(solution)/shard_map/all_to_all | solution.py:82
  106.6 9.8 %fusion.71 = f32[512,512]{1,0:T(8,128)S(1)} fusion(f32[512,2048]{1,0:T(8,128)} %bitcast.1), kind=kOutput, calls=%fused_computation.137 | convolution fusion | flops 6442450944 | bytes 5242880 | tf_op jit(solution)/shard_map/dot_general | solution.py:83
  116.6 1.9 collective-permute-done
  119.9 7.1 %collective-permute-done.1 = f32[128,512]{1,0:T(8,128)S(1)} collective-permute-done((f32[128,512]{1,0:T(8,128)S(1)}, f32[128,512]{1,0:T(8,128)S(1)}, u32[]{:S(2)}, u32[]{:S(2)}) %collective-permute-start.1) | collective-permute-done | bytes 262176 | tf_op jit(solution)/shard_map/ppermute | solution.py:68
  128.3 3.7 %collective-permute-done.2 = f32[64,512]{1,0:T(8,128)S(1)} collective-permute-done((f32[64,512]{1,0:T(8,128)S(1)}, f32[64,512]{1,0:T(8,128)S(1)}, u32[]{:S(2)}, u32[]{:S(2)}) %collective-permute-start.2) | collective-permute-done | bytes 131104 | tf_op jit(solution)/shard_map/ppermute | solution.py:68
  132.2 4.2 %collective-permute-done.3 = f32[32,512]{1,0:T(8,128)S(1)} collective-permute-done((f32[32,512]{1,0:T(8,128)S(1)}, f32[32,512]{1,0:T(8,128)S(1)}, u32[]{:S(2)}, u32[]{:S(2)}) %collective-permute-start.3) | collective-permute-done | bytes 65568 | tf_op jit(solution)/shard_map/ppermute | solution.py:68
  137.1 4.7 %collective-permute-done.4 = f32[16,512]{1,0:T(8,128)S(1)} collective-permute-done((f32[16,512]{1,0:T(8,128)S(1)}, f32[16,512]{1,0:T(8,128)S(1)}, u32[]{:S(2)}, u32[]{:S(2)}) %collective-permute-start.4) | collective-permute-done | bytes 32800 | tf_op jit(solution)/shard_map/ppermute | solution.py:68
  142.3 4.4 %collective-permute-done.5 = f32[16,512]{1,0:T(8,128)S(1)} collective-permute-done((f32[16,512]{1,0:T(8,128)S(1)}, f32[16,512]{1,0:T(8,128)S(1)}, u32[]{:S(2)}, u32[]{:S(2)}) %collective-permute-start.5) | collective-permute-done | bytes 32800 | tf_op jit(solution)/shard_map/ppermute | solution.py:71
  147.1 6.3 %collective-permute-done.6 = f32[32,512]{0,1:T(8,128)S(1)} collective-permute-done((f32[32,512]{0,1:T(8,128)S(1)}, f32[32,512]{0,1:T(8,128)S(1)}, u32[]{:S(2)}, u32[]{:S(2)}) %collective-permute-start.6) | collective-permute-done | bytes 65568 | tf_op jit(solution)/shard_map/ppermute | solution.py:71
  154.9 5.1 %collective-permute-done.7 = f32[64,512]{0,1:T(8,128)S(1)} collective-permute-done((f32[64,512]{0,1:T(8,128)S(1)}, f32[64,512]{0,1:T(8,128)S(1)}, u32[]{:S(2)}, u32[]{:S(2)}) %collective-permute-start.7) | collective-permute-done | bytes 131104 | tf_op jit(solution)/shard_map/ppermute | solution.py:71
  161.6 5.1 %collective-permute-done.8 = f32[128,512]{0,1:T(8,128)S(1)} collective-permute-done((f32[128,512]{0,1:T(8,128)S(1)}, f32[128,512]{0,1:T(8,128)S(1)}, u32[]{:S(2)}, u32[]{:S(2)}) %collective-permute-start.8) | collective-permute-done | bytes 262176 | tf_op jit(solution)/shard_map/ppermute | solution.py:71
  167.0 1.9 collective-permute-done.9
  169.2 11.7 %custom-call.12 = f32[128,128]{1,0:T(8,128)S(1)} custom-call(f32[128,128]{1,0:T(8,128)S(1)} %copy.97), custom_call_target="Cholesky" | custom-call | tf_op jit(solution)/shard_map/cholesky/custom-call.1 | solution.py:15
  182.2 9.8 %custom-call.13 = f32[1,128,128]{1,2,0:T(8,128)S(1)} custom-call(f32[1,128,128]{2,1,0:T(8,128)S(1)} %get-tuple-element.18), custom_call_target="InvertDiagBlocksLowerTriangular" | custom-call | tf_op jit(solution)/shard_map/triangular_solve/custom-call.0 | solution.py:17
  194.5 11.9 %custom-call.14 = f32[128,128]{1,0:T(8,128)S(1)} custom-call(f32[128,128]{1,0:T(8,128)S(1)} %copy.101), custom_call_target="Cholesky" | custom-call | tf_op jit(solution)/shard_map/cholesky/custom-call.1 | solution.py:15
  207.7 9.8 %custom-call.15 = f32[1,128,128]{1,2,0:T(8,128)S(1)} custom-call(f32[1,128,128]{2,1,0:T(8,128)S(1)} %get-tuple-element.16), custom_call_target="InvertDiagBlocksLowerTriangular" | custom-call | tf_op jit(solution)/shard_map/triangular_solve/custom-call.0 | solution.py:17
  218.8 11.7 %custom-call.16 = f32[128,128]{1,0:T(8,128)S(1)} custom-call(f32[128,128]{1,0:T(8,128)S(1)} %fusion.46), custom_call_target="Cholesky" | custom-call | tf_op jit(solution)/shard_map/cholesky/custom-call.1 | solution.py:15
  231.8 9.8 %custom-call.17 = f32[1,128,128]{1,2,0:T(8,128)S(1)} custom-call(f32[1,128,128]{2,1,0:T(8,128)S(1)} %get-tuple-element.14), custom_call_target="InvertDiagBlocksLowerTriangular" | custom-call | tf_op jit(solution)/shard_map/triangular_solve/custom-call.0 | solution.py:17
  245.5 11.7 %custom-call.18 = f32[128,128]{1,0:T(8,128)S(1)} custom-call(f32[128,128]{1,0:T(8,128)S(1)} %broadcast_multiply_fusion), custom_call_target="Cholesky" | custom-call | tf_op jit(solution)/shard_map/cholesky/custom-call.1 | solution.py:15
  258.6 9.8 %custom-call.19 = f32[1,128,128]{1,2,0:T(8,128)S(1)} custom-call(f32[1,128,128]{2,1,0:T(8,128)S(1)} %get-tuple-element.12), custom_call_target="InvertDiagBlocksLowerTriangular" | custom-call | tf_op jit(solution)/shard_map/triangular_solve/custom-call.0 | solution.py:17
  270.5 10.0 %multiply_bitcast_fusion = f32[2048,512]{0,1:T(8,128)} fusion(f32[512,2048]{1,0:T(8,128)} %bitcast.1, f32[128,256]{1,0:T(8,128)S(1)} %broadcast.51, f32[128,128]{1,0:T(8,128)S(1)} %broadcast.64, f32[128,128]{1,0:T(8,128)S(1)} %fusion.38, f32[128,128]{1,0:T(8,128)S(1)} %copy.120, f32[128,128]{1,0:T(8,128)S(1)} %convolution_negate_fusion, ...), kind=kOutput, calls=%fused_computation.1 | convolution fusion | flops 6446907392 | bytes 9240576 | tf_op jit(solution)/shard_map/dot_general | solution.py:92
  280.6 5.3 %copy.122 = f32[2048,512]{1,0:T(8,128)} copy(f32[2048,512]{0,1:T(8,128)} %multiply_bitcast_fusion) | data formatting | bytes 8388608
  (98 shorter events, 24.3 us)
Async XLA Ops:
  5.3 101.3 %all-to-all-start = ((f32[16,32,2048]{2,0,1:T(8,128)}), f32[16,32,2048]{2,0,1:T(8,128)}, u32[]{:S(2)}, u32[]{:S(2)}) async-start(f32[16,32,2048]{2,0,1:T(8,128)} %bitcast.82), calls=%async_computation | async-start | bytes 8388608 | tf_op jit(solution)/shard_map/all_to_all | solution.py:82
  116.5 2.0 collective-permute-start
  118.6 8.4 %collective-permute-start.1 = (f32[128,512]{1,0:T(8,128)S(1)}, f32[128,512]{1,0:T(8,128)S(1)}, u32[]{:S(2)}, u32[]{:S(2)}) collective-permute-start(f32[128,512]{1,0:T(8,128)S(1)} %constant_dynamic-slice_fusion.3), channel_id=1, source_target_pairs={{0,2},{1,3},{2,0},{3,1},{4,6},{5,7},{6,4},{7,5},{8,10},{9,11},{10,... | collective-permute-start | bytes 786440 | tf_op jit(solution)/shard_map/ppermute | solution.py:68
  127.0 5.0 %collective-permute-start.2 = (f32[64,512]{1,0:T(8,128)S(1)}, f32[64,512]{1,0:T(8,128)S(1)}, u32[]{:S(2)}, u32[]{:S(2)}) collective-permute-start(f32[64,512]{1,0:T(8,128)S(1)} %constant_dynamic-slice_fusion.2), channel_id=1, source_target_pairs={{0,4},{1,5},{2,6},{3,7},{4,0},{5,1},{6,2},{7,3},{8,12},{9,13},{10,... | collective-permute-start | bytes 393224 | tf_op jit(solution)/shard_map/ppermute | solution.py:68
  132.1 4.3 %collective-permute-start.3 = (f32[32,512]{1,0:T(8,128)S(1)}, f32[32,512]{1,0:T(8,128)S(1)}, u32[]{:S(2)}, u32[]{:S(2)}) collective-permute-start(f32[32,512]{1,0:T(8,128)S(1)} %constant_dynamic-slice_fusion.1), channel_id=1, source_target_pairs={{0,8},{1,9},{2,10},{3,11},{4,12},{5,13},{6,14},{7,15},{8,0},{9,1},... | collective-permute-start | bytes 196616 | tf_op jit(solution)/shard_map/ppermute | solution.py:68
  136.5 5.4 %collective-permute-start.4 = (f32[16,512]{1,0:T(8,128)S(1)}, f32[16,512]{1,0:T(8,128)S(1)}, u32[]{:S(2)}, u32[]{:S(2)}) collective-permute-start(f32[16,512]{1,0:T(8,128)S(1)} %constant_dynamic-slice_fusion), channel_id=1, source_target_pairs={{0,16},{1,17},{2,18},{3,19},{4,20},{5,21},{6,22},{7,23},{8,24},{9,... | collective-permute-start | bytes 98312 | tf_op jit(solution)/shard_map/ppermute | solution.py:68
  141.9 4.9 %collective-permute-start.5 = (f32[16,512]{1,0:T(8,128)S(1)}, f32[16,512]{1,0:T(8,128)S(1)}, u32[]{:S(2)}, u32[]{:S(2)}) collective-permute-start(f32[16,512]{1,0:T(8,128)S(1)} %dynamic-slice_add_fusion.4), channel_id=1, source_target_pairs={{0,16},{1,17},{2,18},{3,19},{4,20},{5,21},{6,22},{7,23},{8,24},{9,... | collective-permute-start | bytes 98312 | tf_op jit(solution)/shard_map/ppermute | solution.py:71
  146.9 6.4 %collective-permute-start.6 = (f32[32,512]{0,1:T(8,128)S(1)}, f32[32,512]{0,1:T(8,128)S(1)}, u32[]{:S(2)}, u32[]{:S(2)}) collective-permute-start(f32[32,512]{0,1:T(8,128)S(1)} %copy.93), channel_id=1, source_target_pairs={{0,8},{1,9},{2,10},{3,11},{4,12},{5,13},{6,14},{7,15},{8,0},{9,1},... | collective-permute-start | bytes 196616 | tf_op jit(solution)/shard_map/ppermute | solution.py:71
  153.6 6.4 %collective-permute-start.7 = (f32[64,512]{0,1:T(8,128)S(1)}, f32[64,512]{0,1:T(8,128)S(1)}, u32[]{:S(2)}, u32[]{:S(2)}) collective-permute-start(f32[64,512]{0,1:T(8,128)S(1)} %pad_maximum_fusion.6), channel_id=1, source_target_pairs={{0,4},{1,5},{2,6},{3,7},{4,0},{5,1},{6,2},{7,3},{8,12},{9,13},{10,... | collective-permute-start | bytes 393224 | tf_op jit(solution)/shard_map/ppermute | solution.py:71
  160.3 6.4 %collective-permute-start.8 = (f32[128,512]{0,1:T(8,128)S(1)}, f32[128,512]{0,1:T(8,128)S(1)}, u32[]{:S(2)}, u32[]{:S(2)}) collective-permute-start(f32[128,512]{0,1:T(8,128)S(1)} %pad_maximum_fusion.7), channel_id=1, source_target_pairs={{0,2},{1,3},{2,0},{3,1},{4,6},{5,7},{6,4},{7,5},{8,10},{9,11},{10,... | collective-permute-start | bytes 786440 | tf_op jit(solution)/shard_map/ppermute | solution.py:71
  166.9 2.0 collective-permute-start.9
where the time goes:
time: 292 us; the launch traced here: 288 us
  waiting for transfers between devices  138 us (47%)
  other arithmetic  92.6 us (32%)
  matrix products  28 us (10%)
  starting transfers between devices  14.2 us (5%)
  local copies, waits for them, and re-layouts  13.1 us (4%)
    all_to_all x1, waiting for transfers between devices, per_device(): lax.all_to_all(sample_t, AXES, split_axis=1, concat_axis=0, tiled=True)  93.9 us
    another operation x12, other arithmetic, _diag_pair(): lower = lax.linalg.cholesky(block)  49.7 us
    another operation x8, other arithmetic, _diag_pair(): lax.linalg.triangular_solve(lower, identity, left_side=True, lower=True)  41.9 us
    ppermute x5, waiting for transfers between devices, sum_by_halving(): recv = lax.ppermute(buf, AXES, _pair(count, 1 << k))  22.8 us
    ppermute x5, waiting for transfers between devices, sum_by_halving(): buf = keep + lax.ppermute(send, AXES, _pair(count, 1 << k))  21.6 us
    dot_general x1, matrix products, per_device(): lax.dot_general(rows_t, inverse, (((0,), (0,)), ((), ())), precision=lax....  10 us
    dot_general x1, matrix products, per_device(): jnp.dot(rows_t, rows_t.T, precision=lax.Precision.HIGHEST, preferred_elem...  9.77 us
    all_to_all x1, starting transfers between devices, per_device(): lax.all_to_all(sample_t, AXES, split_axis=1, concat_axis=0, tiled=True)  7.43 us
  transfers between devices with their start and end apart: 11, of which 11 were waited for; matrix products, arithmetic and copies ran while one was open for 0% of the time, Pallas kernels for 0%

commit v1 on v0

--- a/solution.py
+++ b/solution.py
@@ -79,7 +79,9 @@
     wide_count = lax.axis_size("wide")
     narrow_count = lax.axis_size("narrow")
     count = wide_count * narrow_count
-    rows_t = lax.all_to_all(sample_t, AXES, split_axis=1, concat_axis=0, tiled=True)
+    pieces = jnp.split(sample_t, lax.axis_size(AXES), axis=1)
+    arrived = lax.all_to_all(jnp.stack(pieces), AXES, 0, 0)
+    rows_t = jnp.concatenate(arrived, axis=0)
     gram_local = jnp.dot(
         rows_t, rows_t.T, precision=lax.Precision.HIGHEST, preferred_element_type=jnp.float32
     )

time: 292 us -> 339 us (1.16)
  local copies, waits for them, and re-layouts: 13.1 us -> 53.2 us
  matrix products: 28 us -> 34.5 us
    unnamed x9 -> x39, local copies, waits for them, and re-layouts: 7.13 us -> 50.4 us
    dot_general x1, matrix products: 10 us -> 16.5 us  [per_device(): lax.dot_general(rows_t, inverse, (((0,), (0,)), ((), ())), precision=lax....]
    all_to_all x1 -> x0, local copies, waits for them, and re-layouts: 4.7 us -> none  [per_device(): lax.all_to_all(sample_t, AXES, split_axis=1, concat_axis=0, tiled=True)]
where the time goes in v1:
time: 339 us; the launch traced here: 334 us
  waiting for transfers between devices  138 us (41%)
  other arithmetic  92.6 us (27%)
  local copies, waits for them, and re-layouts  53.2 us (16%)
  matrix products  34.5 us (10%)
  starting transfers between devices  14.2 us (4%)
    all_to_all x1, waiting for transfers between devices, per_device(): arrived = lax.all_to_all(jnp.stack(pieces), AXES, 0, 0)  93.9 us
    unnamed x39, local copies, waits for them, and re-layouts  50.4 us
    another operation x12, other arithmetic, _diag_pair(): lower = lax.linalg.cholesky(block)  49.7 us
    another operation x8, other arithmetic, _diag_pair(): lax.linalg.triangular_solve(lower, identity, left_side=True, lower=True)  41.9 us
    ppermute x5, waiting for transfers between devices, sum_by_halving(): recv = lax.ppermute(buf, AXES, _pair(count, 1 << k))  22.8 us
    ppermute x5, waiting for transfers between devices, sum_by_halving(): buf = keep + lax.ppermute(send, AXES, _pair(count, 1 << k))  21.7 us
    dot_general x1, matrix products, per_device(): lax.dot_general(rows_t, inverse, (((0,), (0,)), ((), ())), precision=lax....  16.5 us
    dot_general x1, matrix products, per_device(): jnp.dot(rows_t, rows_t.T, precision=lax.Precision.HIGHEST, preferred_elem...  9.83 us
  transfers between devices with their start and end apart: 11, of which 11 were waited for; matrix products, arithmetic and copies ran while one was open for 0% of the time, Pallas kernels for 0%

profile of v1, /device:TPU:0, one launch (start us, length us, event | category | flops | bytes accessed | tf_op | source)
XLA Modules:
  0.0 334.4 jit_solution(11222898714630203223)
XLA Ops:
  0.6 1.6 bitcast_dynamic-update-slice_fusion.31
  3.8 1.6 bitcast_dynamic-update-slice_fusion.29
  50.8 7.4 %all-to-all-start = ((f32[32,16,2048]{2,1,0:T(8,128)}), f32[32,16,2048]{2,1,0:T(8,128)}, u32[]{:S(2)}, u32[]{:S(2)}) async-start(f32[32,16,2048]{2,1,0:T(8,128)} %bitcast_dynamic-update-slice_fusion), calls=%async_computation | async-start | bytes 8388608 | tf_op jit(solution)/shard_map/all_to_all | solution.py:83
  58.2 93.9 %all-to-all-done = f32[32,16,2048]{2,1,0:T(8,128)} async-done(((f32[32,16,2048]{2,1,0:T(8,128)}), f32[32,16,2048]{2,1,0:T(8,128)}, u32[]{:S(2)}, u32[]{:S(2)}) %all-to-all-start) | async-done | bytes 4194336 | tf_op jit(solution)/shard_map/all_to_all | solution.py:83
  152.1 9.8 %fusion.71 = f32[512,512]{1,0:T(8,128)S(1)} fusion(f32[512,2048]{1,0:T(8,128)} %bitcast.32), kind=kOutput, calls=%fused_computation.168 | convolution fusion | flops 6442450944 | bytes 5242880 | tf_op jit(solution)/shard_map/dot_general | solution.py:85
  162.1 1.9 collective-permute-done
  165.4 7.1 %collective-permute-done.1 = f32[128,512]{1,0:T(8,128)S(1)} collective-permute-done((f32[128,512]{1,0:T(8,128)S(1)}, f32[128,512]{1,0:T(8,128)S(1)}, u32[]{:S(2)}, u32[]{:S(2)}) %collective-permute-start.1) | collective-permute-done | bytes 262176 | tf_op jit(solution)/shard_map/ppermute | solution.py:68
  173.9 3.7 %collective-permute-done.2 = f32[64,512]{1,0:T(8,128)S(1)} collective-permute-done((f32[64,512]{1,0:T(8,128)S(1)}, f32[64,512]{1,0:T(8,128)S(1)}, u32[]{:S(2)}, u32[]{:S(2)}) %collective-permute-start.2) | collective-permute-done | bytes 131104 | tf_op jit(solution)/shard_map/ppermute | solution.py:68
  177.7 4.2 %collective-permute-done.3 = f32[32,512]{1,0:T(8,128)S(1)} collective-permute-done((f32[32,512]{1,0:T(8,128)S(1)}, f32[32,512]{1,0:T(8,128)S(1)}, u32[]{:S(2)}, u32[]{:S(2)}) %collective-permute-start.3) | collective-permute-done | bytes 65568 | tf_op jit(solution)/shard_map/ppermute | solution.py:68
  182.7 4.7 %collective-permute-done.4 = f32[16,512]{1,0:T(8,128)S(1)} collective-permute-done((f32[16,512]{1,0:T(8,128)S(1)}, f32[16,512]{1,0:T(8,128)S(1)}, u32[]{:S(2)}, u32[]{:S(2)}) %collective-permute-start.4) | collective-permute-done | bytes 32800 | tf_op jit(solution)/shard_map/ppermute | solution.py:68
  187.9 4.4 %collective-permute-done.5 = f32[16,512]{1,0:T(8,128)S(1)} collective-permute-done((f32[16,512]{1,0:T(8,128)S(1)}, f32[16,512]{1,0:T(8,128)S(1)}, u32[]{:S(2)}, u32[]{:S(2)}) %collective-permute-start.5) | collective-permute-done | bytes 32800 | tf_op jit(solution)/shard_map/ppermute | solution.py:71
  192.6 6.3 %collective-permute-done.6 = f32[32,512]{0,1:T(8,128)S(1)} collective-permute-done((f32[32,512]{0,1:T(8,128)S(1)}, f32[32,512]{0,1:T(8,128)S(1)}, u32[]{:S(2)}, u32[]{:S(2)}) %collective-permute-start.6) | collective-permute-done | bytes 65568 | tf_op jit(solution)/shard_map/ppermute | solution.py:71
  200.4 5.1 %collective-permute-done.7 = f32[64,512]{0,1:T(8,128)S(1)} collective-permute-done((f32[64,512]{0,1:T(8,128)S(1)}, f32[64,512]{0,1:T(8,128)S(1)}, u32[]{:S(2)}, u32[]{:S(2)}) %collective-permute-start.7) | collective-permute-done | bytes 131104 | tf_op jit(solution)/shard_map/ppermute | solution.py:71
  207.2 5.1 %collective-permute-done.8 = f32[128,512]{0,1:T(8,128)S(1)} collective-permute-done((f32[128,512]{0,1:T(8,128)S(1)}, f32[128,512]{0,1:T(8,128)S(1)}, u32[]{:S(2)}, u32[]{:S(2)}) %collective-permute-start.8) | collective-permute-done | bytes 262176 | tf_op jit(solution)/shard_map/ppermute | solution.py:71
  212.5 1.9 collective-permute-done.9
  214.7 11.7 %custom-call.12 = f32[128,128]{1,0:T(8,128)S(1)} custom-call(f32[128,128]{1,0:T(8,128)S(1)} %copy.35), custom_call_target="Cholesky" | custom-call | tf_op jit(solution)/shard_map/cholesky/custom-call.1 | solution.py:15
  227.8 9.8 %custom-call.13 = f32[1,128,128]{1,2,0:T(8,128)S(1)} custom-call(f32[1,128,128]{2,1,0:T(8,128)S(1)} %get-tuple-element.14), custom_call_target="InvertDiagBlocksLowerTriangular" | custom-call | tf_op jit(solution)/shard_map/triangular_solve/custom-call.0 | solution.py:17
  240.0 11.9 %custom-call.14 = f32[128,128]{1,0:T(8,128)S(1)} custom-call(f32[128,128]{1,0:T(8,128)S(1)} %copy.39), custom_call_target="Cholesky" | custom-call | tf_op jit(solution)/shard_map/cholesky/custom-call.1 | solution.py:15
  253.2 9.8 %custom-call.15 = f32[1,128,128]{1,2,0:T(8,128)S(1)} custom-call(f32[1,128,128]{2,1,0:T(8,128)S(1)} %get-tuple-element.12), custom_call_target="InvertDiagBlocksLowerTriangular" | custom-call | tf_op jit(solution)/shard_map/triangular_solve/custom-call.0 | solution.py:17
  264.3 11.7 %custom-call.16 = f32[128,128]{1,0:T(8,128)S(1)} custom-call(f32[128,128]{1,0:T(8,128)S(1)} %fusion.46), custom_call_target="Cholesky" | custom-call | tf_op jit(solution)/shard_map/cholesky/custom-call.1 | solution.py:15
  277.4 9.8 %custom-call.17 = f32[1,128,128]{1,2,0:T(8,128)S(1)} custom-call(f32[1,128,128]{2,1,0:T(8,128)S(1)} %get-tuple-element.10), custom_call_target="InvertDiagBlocksLowerTriangular" | custom-call | tf_op jit(solution)/shard_map/triangular_solve/custom-call.0 | solution.py:17
  291.0 11.7 %custom-call.18 = f32[128,128]{1,0:T(8,128)S(1)} custom-call(f32[128,128]{1,0:T(8,128)S(1)} %broadcast_multiply_fusion), custom_call_target="Cholesky" | custom-call | tf_op jit(solution)/shard_map/cholesky/custom-call.1 | solution.py:15
  304.1 9.8 %custom-call.19 = f32[1,128,128]{1,2,0:T(8,128)S(1)} custom-call(f32[1,128,128]{2,1,0:T(8,128)S(1)} %get-tuple-element.8), custom_call_target="InvertDiagBlocksLowerTriangular" | custom-call | tf_op jit(solution)/shard_map/triangular_solve/custom-call.0 | solution.py:17
  317.7 16.5 %convolution_multiply_fusion = f32[2048,512]{1,0:T(8,128)} fusion(f32[512,2048]{1,0:T(8,128)} %bitcast.32, f32[128,256]{1,0:T(8,128)S(1)} %broadcast.49, f32[128,128]{1,0:T(8,128)S(1)} %broadcast.62, f32[128,128]{1,0:T(8,128)S(1)} %fusion.38, f32[128,128]{1,0:T(8,128)S(1)} %copy.55, f32[128,128]{1,0:T(8,128)S(1)} %convolution_negate_fusion, ...), kind=kOutput, calls=%fused_computation | convolution fusion | flops 6446907392 | bytes 9240576 | tf_op jit(solution)/shard_map/dot_general | solution.py:94
  (128 shorter events, 71.4 us)
Async XLA Ops:
  50.8 101.3 %all-to-all-start = ((f32[32,16,2048]{2,1,0:T(8,128)}), f32[32,16,2048]{2,1,0:T(8,128)}, u32[]{:S(2)}, u32[]{:S(2)}) async-start(f32[32,16,2048]{2,1,0:T(8,128)} %bitcast_dynamic-update-slice_fusion), calls=%async_computation | async-start | bytes 8388608 | tf_op jit(solution)/shard_map/all_to_all | solution.py:83
  162.0 2.0 collective-permute-start
  164.1 8.4 %collective-permute-start.1 = (f32[128,512]{1,0:T(8,128)S(1)}, f32[128,512]{1,0:T(8,128)S(1)}, u32[]{:S(2)}, u32[]{:S(2)}) collective-permute-start(f32[128,512]{1,0:T(8,128)S(1)} %constant_dynamic-slice_fusion.3), channel_id=1, source_target_pairs={{0,2},{1,3},{2,0},{3,1},{4,6},{5,7},{6,4},{7,5},{8,10},{9,11},{10,... | collective-permute-start | bytes 786440 | tf_op jit(solution)/shard_map/ppermute | solution.py:68
  172.6 5.0 %collective-permute-start.2 = (f32[64,512]{1,0:T(8,128)S(1)}, f32[64,512]{1,0:T(8,128)S(1)}, u32[]{:S(2)}, u32[]{:S(2)}) collective-permute-start(f32[64,512]{1,0:T(8,128)S(1)} %constant_dynamic-slice_fusion.2), channel_id=1, source_target_pairs={{0,4},{1,5},{2,6},{3,7},{4,0},{5,1},{6,2},{7,3},{8,12},{9,13},{10,... | collective-permute-start | bytes 393224 | tf_op jit(solution)/shard_map/ppermute | solution.py:68
  177.7 4.3 %collective-permute-start.3 = (f32[32,512]{1,0:T(8,128)S(1)}, f32[32,512]{1,0:T(8,128)S(1)}, u32[]{:S(2)}, u32[]{:S(2)}) collective-permute-start(f32[32,512]{1,0:T(8,128)S(1)} %constant_dynamic-slice_fusion.1), channel_id=1, source_target_pairs={{0,8},{1,9},{2,10},{3,11},{4,12},{5,13},{6,14},{7,15},{8,0},{9,1},... | collective-permute-start | bytes 196616 | tf_op jit(solution)/shard_map/ppermute | solution.py:68
  182.0 5.4 %collective-permute-start.4 = (f32[16,512]{1,0:T(8,128)S(1)}, f32[16,512]{1,0:T(8,128)S(1)}, u32[]{:S(2)}, u32[]{:S(2)}) collective-permute-start(f32[16,512]{1,0:T(8,128)S(1)} %constant_dynamic-slice_fusion), channel_id=1, source_target_pairs={{0,16},{1,17},{2,18},{3,19},{4,20},{5,21},{6,22},{7,23},{8,24},{9,... | collective-permute-start | bytes 98312 | tf_op jit(solution)/shard_map/ppermute | solution.py:68
  187.4 4.9 %collective-permute-start.5 = (f32[16,512]{1,0:T(8,128)S(1)}, f32[16,512]{1,0:T(8,128)S(1)}, u32[]{:S(2)}, u32[]{:S(2)}) collective-permute-start(f32[16,512]{1,0:T(8,128)S(1)} %dynamic-slice_add_fusion.4), channel_id=1, source_target_pairs={{0,16},{1,17},{2,18},{3,19},{4,20},{5,21},{6,22},{7,23},{8,24},{9,... | collective-permute-start | bytes 98312 | tf_op jit(solution)/shard_map/ppermute | solution.py:71
  192.5 6.4 %collective-permute-start.6 = (f32[32,512]{0,1:T(8,128)S(1)}, f32[32,512]{0,1:T(8,128)S(1)}, u32[]{:S(2)}, u32[]{:S(2)}) collective-permute-start(f32[32,512]{0,1:T(8,128)S(1)} %copy.31), channel_id=1, source_target_pairs={{0,8},{1,9},{2,10},{3,11},{4,12},{5,13},{6,14},{7,15},{8,0},{9,1},... | collective-permute-start | bytes 196616 | tf_op jit(solution)/shard_map/ppermute | solution.py:71
  199.1 6.4 %collective-permute-start.7 = (f32[64,512]{0,1:T(8,128)S(1)}, f32[64,512]{0,1:T(8,128)S(1)}, u32[]{:S(2)}, u32[]{:S(2)}) collective-permute-start(f32[64,512]{0,1:T(8,128)S(1)} %pad_maximum_fusion.6), channel_id=1, source_target_pairs={{0,4},{1,5},{2,6},{3,7},{4,0},{5,1},{6,2},{7,3},{8,12},{9,13},{10,... | collective-permute-start | bytes 393224 | tf_op jit(solution)/shard_map/ppermute | solution.py:71
  205.8 6.4 %collective-permute-start.8 = (f32[128,512]{0,1:T(8,128)S(1)}, f32[128,512]{0,1:T(8,128)S(1)}, u32[]{:S(2)}, u32[]{:S(2)}) collective-permute-start(f32[128,512]{0,1:T(8,128)S(1)} %pad_maximum_fusion.7), channel_id=1, source_target_pairs={{0,2},{1,3},{2,0},{3,1},{4,6},{5,7},{6,4},{7,5},{8,10},{9,11},{10,... | collective-permute-start | bytes 786440 | tf_op jit(solution)/shard_map/ppermute | solution.py:71
  212.4 2.0 collective-permute-start.9
